TPU v7x, 256 devices: a whole 4x4x8 slice. The times are simulated.
256 devices in a mesh: leaf: 4 (over x), row: 4 (over y), col: 16 (over z, core).
Axes of the slice: x: 4, y: 4, z: 8, core: 2. Of those that a mesh axis runs over, the one named last changes fastest.
Arguments:
- local_inv: float32 [4, 4, 256, 128, 128], P('leaf', 'row', 'col'), may hold values from -2 to 2, as said below
- local_off: float32 [4, 4, 256, 2, 128, 128], P('leaf', 'row', 'col'), may hold values from -0.09375 to 0.09375
- local_dep: int32 [4, 4, 256, 2], P('leaf', 'row', 'col'), may hold values from 0 to 7
- local_rhs: float32 [4, 4, 256, 64, 128], P('leaf', 'row', 'col'), may hold values from -6 to 6
- top_inv: float32 [8, 4, 16, 128, 128], P(None, 'row', 'col'), may hold values from -2 to 2, as said below
- top_off: float32 [7, 4, 16, 4, 128, 128], P(None, 'row', 'col'), may hold values from -0.125 to 0.125
- top_dep: int32 [7, 4, 16, 4], P(None, 'row', 'col'), may hold values from 0 to 19
- top_rhs: float32 [8, 4, 16, 64, 128], P(None, 'row', 'col'), may hold values from -6 to 6
Outputs:
- local_sol: float32 [4, 4, 256, 64, 128], P('leaf', 'row', 'col')
- top_sol: float32 [8, 4, 16, 64, 128], P(None, 'row', 'col')
Inputs may be any that keep to these rules, and one draw needn't show every extreme that they name: `local_inv`: lower-triangular inverse diagonal blocks of a Cholesky factor: entry [t, s] is zero for s > t. `top_inv`: lower-triangular inverse diagonal blocks of a Cholesky factor: entry [t, s] is zero for s > t. `local_dep`: levels of ancestors owned by the supernode's own grid cell. `top_dep`: a value v < 16 names the supernode one level lower in cell (r, v); a value v >= 16 the one in cell (v - 16, c).
All inputs are finite; a program needn't handle non-finite values.
Results may differ from a plain program's by a relative error of at most 0.0001.
Values sent between devices are 32-bit elements; how exact they have to be, the bound alone decides.
No kernel may reach another device: no remote copies, remote signals or barrier semaphores. Data moves between devices by JAX's collectives and lax.ppermute only.
A program may use at most 64 MiB of HBM per device.

v0:
```python
import jax
import jax.numpy as jnp
from jax import lax
from jax.sharding import PartitionSpec as P

highest = lax.Precision.HIGHEST


def apply_inverse(inverse, block):
    return jnp.einsum("rs,ts->rt", block, inverse, precision=highest)


def apply_transpose(inverse, block):
    return jnp.einsum("rs,st->rt", block, inverse, precision=highest)


def shifted(value, axis, k):
    n = lax.axis_size(axis)
    return lax.ppermute(value, axis, [(i, (i + k) % n) for i in range(n)])


def select_sum(mask, stacked):
    mask = mask.reshape(mask.shape + (1,) * (stacked.ndim - 1))
    return jnp.sum(jnp.where(mask, stacked[None], 0.0), axis=1)


def spread_sum(mask, pieces):
    return jnp.sum(jnp.where(mask[:, :, None, None], pieces[:, None], 0.0), axis=0)


def gather_sources(block, col_pick, row_pick):
    by_col = lax.all_gather(block[None], "col", axis=0, tiled=True)
    n_row = lax.axis_size("row")
    by_shift = jnp.stack([block] + [shifted(block, "row", k) for k in range(1, n_row)])
    return select_sum(col_pick, by_col) + select_sum(row_pick, by_shift)


def push_back(pieces, col_pick, row_push):
    n_row = lax.axis_size("row")
    slots = spread_sum(col_pick, pieces)
    incoming = lax.all_to_all(slots, "col", 0, 0, tiled=True).sum(0)
    parts = spread_sum(row_push, pieces)
    incoming = incoming + parts[0]
    for k in range(1, n_row):
        incoming = incoming + shifted(parts[k], "row", k)
    return incoming


def solve_top(top_inverse, top_blocks, top_links, top_right, updates):
    levels = top_inverse.shape[0]
    width_cols = lax.axis_size("col")
    n_row = lax.axis_size("row")
    me_row = lax.axis_index("row")
    is_col = top_links < width_cols
    col_pick = top_links[..., None] == jnp.arange(width_cols, dtype=jnp.int32)
    pull = jnp.mod(me_row - (top_links - width_cols), n_row)
    push = jnp.mod(top_links - width_cols - me_row, n_row)
    shifts = jnp.arange(n_row, dtype=jnp.int32)
    row_pick = (~is_col)[..., None] & (pull[..., None] == shifts)
    row_push = (~is_col)[..., None] & (push[..., None] == shifts)
    forward = []
    for height in range(levels):
        target = top_right[height] - updates[height]
        if height > 0:
            picked = gather_sources(forward[-1], col_pick[height - 1], row_pick[height - 1])
            target = target - jnp.einsum(
                "jrs,jts->rt", picked, top_blocks[height - 1], precision=highest
            )
        forward.append(apply_inverse(top_inverse[height], target))
    forward = jnp.stack(forward)
    current = apply_transpose(top_inverse[levels - 1], forward[levels - 1])
    solved = jnp.zeros_like(forward).at[levels - 1].set(current)

    def step(i, carry):
        current, solved = carry
        height = levels - 2 - i
        at = lambda a: lax.dynamic_index_in_dim(a, height, 0, keepdims=False)
        pieces = jnp.einsum("rt,jts->jrs", current, at(top_blocks), precision=highest)
        incoming = push_back(pieces, at(col_pick), at(row_push))
        current = apply_transpose(at(top_inverse), at(forward) - incoming)
        return (current, lax.dynamic_update_index_in_dim(solved, current, height, 0))

    return lax.fori_loop(0, levels - 1, step, (current, solved))[1]


def on_device(local_inv, local_off, local_dep, local_rhs, top_inv, top_off, top_dep, top_rhs):
    inverse = local_inv[0, 0]
    blocks = local_off[0, 0]
    ancestor_levels = local_dep[0, 0]
    right_local = local_rhs[0, 0]
    levels = top_inv.shape[0]
    top_inverse = top_inv[:, 0, 0]
    top_blocks = top_off[:, 0, 0]
    top_links = top_dep[:, 0, 0]
    top_right = top_rhs[:, 0, 0]
    local_first = jnp.einsum("krs,kts->krt", right_local, inverse, precision=highest)
    contributions = jnp.einsum("krs,kjts->kjrt", local_first, blocks, precision=highest)
    level_matches = (ancestor_levels[:, :, None] == jnp.arange(levels, dtype=jnp.int32)).astype(
        jnp.float32
    )
    updates = jnp.einsum("kjl,kjrt->lrt", level_matches, contributions, precision=highest)
    n_leaf = lax.axis_size("leaf")
    by_shift = jnp.stack([updates] + [shifted(updates, "leaf", k) for k in range(1, n_leaf)])
    order = jnp.mod(lax.axis_index("leaf") - jnp.arange(n_leaf, dtype=jnp.int32), n_leaf)
    weights = order[:, None] == jnp.arange(n_leaf, dtype=jnp.int32)
    ordered = select_sum(weights, by_shift)
    totals = ordered[0]
    for u in range(1, n_leaf):
        totals = totals + ordered[u]
    top_solution = solve_top(top_inverse, top_blocks, top_links, top_right, totals)
    ancestors = jnp.einsum("kjl,lrt->kjrt", level_matches, top_solution, precision=highest)
    remainder = local_first - jnp.einsum("kjrt,kjts->krs", ancestors, blocks, precision=highest)
    local_solution = jnp.einsum("krs,kst->krt", remainder, inverse, precision=highest)
    return (local_solution[None, None], top_solution[:, None, None])


def solution(mesh):
    placed = (
        P("leaf", "row", "col", None, None),
        P("leaf", "row", "col", None, None, None),
        P("leaf", "row", "col", None),
        P("leaf", "row", "col", None, None),
        P(None, "row", "col", None, None),
        P(None, "row", "col", None, None, None),
        P(None, "row", "col", None),
        P(None, "row", "col", None, None),
    )
    return jax.shard_map(
        on_device,
        mesh=mesh,
        in_specs=placed,
        out_specs=(P("leaf", "row", "col", None, None), P(None, "row", "col", None, None)),
        check_vma=False,
    )
```

profile of v0, /device:TPU:1, one launch (start us, length us, event | category | flops | bytes accessed | tf_op | source)
XLA Modules:
  0.0 378.8 jit_solution(4697018135431169076)
XLA Ops:
  0.6 3.7 fusion.36
  14.9 8.8 %collective-permute-done.4 = f32[8,64,128]{2,0,1:T(8,128)S(1)} collective-permute-done((f32[8,64,128]{2,0,1:T(8,128)S(1)}, f32[8,64,128]{2,0,1:T(8,128)S(1)}, u32[]{:S(2)}, u32[]{:S(2)}) %collective-permute-start.4) | collective-permute-done | bytes 262176 | tf_op jit(solution)/shard_map/ppermute | solution.py:19
  31.6 23.6 %all-gather = f32[1024,128]{1,0:T(8,128)S(1)} all-gather(f32[64,128]{1,0:T(8,128)S(1)} %get-tuple-element.254), channel_id=2, replica_groups=mesh['leaf'=4,'row'=4,'col'=16] {'col'}, dimensions={0}, use_global_device_ids=true | all-gather | bytes 557056 | tf_op jit(solution)/shard_map/all_gather | solution.py:32
  61.0 16.3 %all-gather.1 = f32[1024,128]{1,0:T(8,128)S(1)} all-gather(f32[64,128]{1,0:T(8,128)S(1)} %get-tuple-element.256), channel_id=3, replica_groups=mesh['leaf'=4,'row'=4,'col'=16] {'col'}, dimensions={0}, use_global_device_ids=true | all-gather | bytes 557056 | tf_op jit(solution)/shard_map/all_gather | solution.py:32
  84.7 18.2 %all-gather.2 = f32[1024,128]{1,0:T(8,128)S(1)} all-gather(f32[64,128]{1,0:T(8,128)S(1)} %get-tuple-element.258), channel_id=4, replica_groups=mesh['leaf'=4,'row'=4,'col'=16] {'col'}, dimensions={0}, use_global_device_ids=true | all-gather | bytes 557056 | tf_op jit(solution)/shard_map/all_gather | solution.py:32
  108.5 16.5 %all-gather.3 = f32[1024,128]{1,0:T(8,128)S(1)} all-gather(f32[64,128]{1,0:T(8,128)S(1)} %get-tuple-element.260), channel_id=5, replica_groups=mesh['leaf'=4,'row'=4,'col'=16] {'col'}, dimensions={0}, use_global_device_ids=true | all-gather | bytes 557056 | tf_op jit(solution)/shard_map/all_gather | solution.py:32
  132.4 18.2 %all-gather.4 = f32[1024,128]{1,0:T(8,128)S(1)} all-gather(f32[64,128]{1,0:T(8,128)S(1)} %get-tuple-element.262), channel_id=6, replica_groups=mesh['leaf'=4,'row'=4,'col'=16] {'col'}, dimensions={0}, use_global_device_ids=true | all-gather | bytes 557056 | tf_op jit(solution)/shard_map/all_gather | solution.py:32
  156.3 16.7 %all-gather.5 = f32[1024,128]{1,0:T(8,128)S(1)} all-gather(f32[64,128]{1,0:T(8,128)S(1)} %get-tuple-element.264), channel_id=7, replica_groups=mesh['leaf'=4,'row'=4,'col'=16] {'col'}, dimensions={0}, use_global_device_ids=true | all-gather | bytes 557056 | tf_op jit(solution)/shard_map/all_gather | solution.py:32
  180.4 18.2 %all-gather.6 = f32[1024,128]{1,0:T(8,128)S(1)} all-gather(f32[64,128]{1,0:T(8,128)S(1)} %get-tuple-element.266), channel_id=8, replica_groups=mesh['leaf'=4,'row'=4,'col'=16] {'col'}, dimensions={0}, use_global_device_ids=true | all-gather | bytes 557056 | tf_op jit(solution)/shard_map/all_gather | solution.py:32
  203.3 170.0 %while.18 = (s32[]{:T(128)}, f32[64,128]{1,0:T(8,128)S(1)}, f32[8,64,128]{2,1,0:T(8,128)}, f32[8,64,128]{2,1,0:T(8,128)}, pred[7,4,16]{2,1,0:T(4,128)(4,1)S(1)},...) while((s32[]{:T(128)}, f32[64,128]{1,0:T(8,128)S(1)}, ...), condition=%wide.region_19.20_spmd, body=%wide.region_15.19_spmd.sunk | while | flops 64225288 | bytes 4393060 | solution.py:83
  205.5 3.8 %all-to-all-start = ((f32[16,64,128]{2,1,0:T(8,128)}), f32[16,64,128]{2,1,0:T(8,128)S(1)}, u32[]{:S(2)}, u32[]{:S(2)}) async-start(f32[16,64,128]{2,1,0:T(8,128)} %select_reduce_fusion.20), calls=%async_computation | async-start | bytes 1048576 | tf_op jit(solution)/shard_map/while/body/eval_jaxpr/all_to_all | solution.py:41
  211.0 15.5 %all-to-all-done = f32[16,64,128]{2,1,0:T(8,128)S(1)} async-done(((f32[16,64,128]{2,1,0:T(8,128)}), f32[16,64,128]{2,1,0:T(8,128)S(1)}, u32[]{:S(2)}, u32[]{:S(2)}) %all-to-all-start) | async-done | bytes 524320 | tf_op jit(solution)/shard_map/while/body/eval_jaxpr/all_to_all | solution.py:41
  230.5 3.5 all-to-all-start
  235.7 15.0 %all-to-all-done = f32[16,64,128]{2,1,0:T(8,128)S(1)} async-done(((f32[16,64,128]{2,1,0:T(8,128)}), f32[16,64,128]{2,1,0:T(8,128)S(1)}, u32[]{:S(2)}, u32[]{:S(2)}) %all-to-all-start) | async-done | bytes 524320 | tf_op jit(solution)/shard_map/while/body/eval_jaxpr/all_to_all | solution.py:41
  254.7 3.5 all-to-all-start
  259.9 15.0 %all-to-all-done = f32[16,64,128]{2,1,0:T(8,128)S(1)} async-done(((f32[16,64,128]{2,1,0:T(8,128)}), f32[16,64,128]{2,1,0:T(8,128)S(1)}, u32[]{:S(2)}, u32[]{:S(2)}) %all-to-all-start) | async-done | bytes 524320 | tf_op jit(solution)/shard_map/while/body/eval_jaxpr/all_to_all | solution.py:41
  278.9 3.5 all-to-all-start
  284.0 15.0 %all-to-all-done = f32[16,64,128]{2,1,0:T(8,128)S(1)} async-done(((f32[16,64,128]{2,1,0:T(8,128)}), f32[16,64,128]{2,1,0:T(8,128)S(1)}, u32[]{:S(2)}, u32[]{:S(2)}) %all-to-all-start) | async-done | bytes 524320 | tf_op jit(solution)/shard_map/while/body/eval_jaxpr/all_to_all | solution.py:41
  303.0 3.5 all-to-all-start
  308.2 15.0 %all-to-all-done = f32[16,64,128]{2,1,0:T(8,128)S(1)} async-done(((f32[16,64,128]{2,1,0:T(8,128)}), f32[16,64,128]{2,1,0:T(8,128)S(1)}, u32[]{:S(2)}, u32[]{:S(2)}) %all-to-all-start) | async-done | bytes 524320 | tf_op jit(solution)/shard_map/while/body/eval_jaxpr/all_to_all | solution.py:41
  327.2 3.5 all-to-all-start
  332.4 15.0 %all-to-all-done = f32[16,64,128]{2,1,0:T(8,128)S(1)} async-done(((f32[16,64,128]{2,1,0:T(8,128)}), f32[16,64,128]{2,1,0:T(8,128)S(1)}, u32[]{:S(2)}, u32[]{:S(2)}) %all-to-all-start) | async-done | bytes 524320 | tf_op jit(solution)/shard_map/while/body/eval_jaxpr/all_to_all | solution.py:41
  351.4 3.5 all-to-all-start
  356.5 15.0 %all-to-all-done = f32[16,64,128]{2,1,0:T(8,128)S(1)} async-done(((f32[16,64,128]{2,1,0:T(8,128)}), f32[16,64,128]{2,1,0:T(8,128)S(1)}, u32[]{:S(2)}, u32[]{:S(2)}) %all-to-all-start) | async-done | bytes 524320 | tf_op jit(solution)/shard_map/while/body/eval_jaxpr/all_to_all | solution.py:41
  (216 shorter events, 106.5 us)
Async XLA Ops:
  26.5 28.9 %collective-permute-start.6 = (f32[64,128]{1,0:T(8,128)S(1)}, f32[64,128]{1,0:T(8,128)S(1)}, u32[]{:S(2)}, u32[]{:S(2)}) collective-permute-start(f32[64,128]{1,0:T(8,128)S(1)} %get-tuple-element.254), channel_id=1, source_target_pairs={{0,16},{16,32},{32,48},{48,0},{1,17},{17,33},{33,49},{49,1},{2,18}... | collective-permute-start | bytes 98312 | tf_op jit(solution)/shard_map/ppermute | solution.py:19
  27.9 27.5 %collective-permute-start.7 = (f32[64,128]{1,0:T(8,128)S(1)}, f32[64,128]{1,0:T(8,128)S(1)}, u32[]{:S(2)}, u32[]{:S(2)}) collective-permute-start(f32[64,128]{1,0:T(8,128)S(1)} %get-tuple-element.254), channel_id=1, source_target_pairs={{0,32},{16,48},{32,0},{48,16},{1,33},{17,49},{33,1},{49,17},{2,34}... | collective-permute-start | bytes 98312 | tf_op jit(solution)/shard_map/ppermute | solution.py:19
  30.5 24.9 %collective-permute-start.8 = (f32[64,128]{1,0:T(8,128)S(1)}, f32[64,128]{1,0:T(8,128)S(1)}, u32[]{:S(2)}, u32[]{:S(2)}) collective-permute-start(f32[64,128]{1,0:T(8,128)S(1)} %get-tuple-element.254), channel_id=1, source_target_pairs={{0,48},{16,0},{32,16},{48,32},{1,49},{17,1},{33,17},{49,33},{2,50}... | collective-permute-start | bytes 98312 | tf_op jit(solution)/shard_map/ppermute | solution.py:19
  58.1 19.5 %collective-permute-start.9 = (f32[64,128]{1,0:T(8,128)S(1)}, f32[64,128]{1,0:T(8,128)S(1)}, u32[]{:S(2)}, u32[]{:S(2)}) collective-permute-start(f32[64,128]{1,0:T(8,128)S(1)} %get-tuple-element.256), channel_id=1, source_target_pairs={{0,16},{16,32},{32,48},{48,0},{1,17},{17,33},{33,49},{49,1},{2,18}... | collective-permute-start | bytes 98312 | tf_op jit(solution)/shard_map/ppermute | solution.py:19
  80.1 23.0 %collective-permute-start.12 = (f32[64,128]{1,0:T(8,128)S(1)}, f32[64,128]{1,0:T(8,128)S(1)}, u32[]{:S(2)}, u32[]{:S(2)}) collective-permute-start(f32[64,128]{1,0:T(8,128)S(1)} %get-tuple-element.258), channel_id=1, source_target_pairs={{0,16},{16,32},{32,48},{48,0},{1,17},{17,33},{33,49},{49,1},{2,18}... | collective-permute-start | bytes 98312 | tf_op jit(solution)/shard_map/ppermute | solution.py:19
  80.6 22.6 %collective-permute-start.13 = (f32[64,128]{1,0:T(8,128)S(1)}, f32[64,128]{1,0:T(8,128)S(1)}, u32[]{:S(2)}, u32[]{:S(2)}) collective-permute-start(f32[64,128]{1,0:T(8,128)S(1)} %get-tuple-element.258), channel_id=1, source_target_pairs={{0,32},{16,48},{32,0},{48,16},{1,33},{17,49},{33,1},{49,17},{2,34}... | collective-permute-start | bytes 98312 | tf_op jit(solution)/shard_map/ppermute | solution.py:19
  82.7 20.4 %collective-permute-start.14 = (f32[64,128]{1,0:T(8,128)S(1)}, f32[64,128]{1,0:T(8,128)S(1)}, u32[]{:S(2)}, u32[]{:S(2)}) collective-permute-start(f32[64,128]{1,0:T(8,128)S(1)} %get-tuple-element.258), channel_id=1, source_target_pairs={{0,48},{16,0},{32,16},{48,32},{1,49},{17,1},{33,17},{49,33},{2,50}... | collective-permute-start | bytes 98312 | tf_op jit(solution)/shard_map/ppermute | solution.py:19
  105.8 19.5 %collective-permute-start.15 = (f32[64,128]{1,0:T(8,128)S(1)}, f32[64,128]{1,0:T(8,128)S(1)}, u32[]{:S(2)}, u32[]{:S(2)}) collective-permute-start(f32[64,128]{1,0:T(8,128)S(1)} %get-tuple-element.260), channel_id=1, source_target_pairs={{0,16},{16,32},{32,48},{48,0},{1,17},{17,33},{33,49},{49,1},{2,18}... | collective-permute-start | bytes 98312 | tf_op jit(solution)/shard_map/ppermute | solution.py:19
  105.9 19.4 %collective-permute-start.16 = (f32[64,128]{1,0:T(8,128)S(1)}, f32[64,128]{1,0:T(8,128)S(1)}, u32[]{:S(2)}, u32[]{:S(2)}) collective-permute-start(f32[64,128]{1,0:T(8,128)S(1)} %get-tuple-element.260), channel_id=1, source_target_pairs={{0,32},{16,48},{32,0},{48,16},{1,33},{17,49},{33,1},{49,17},{2,34}... | collective-permute-start | bytes 98312 | tf_op jit(solution)/shard_map/ppermute | solution.py:19
  127.9 23.0 %collective-permute-start.18 = (f32[64,128]{1,0:T(8,128)S(1)}, f32[64,128]{1,0:T(8,128)S(1)}, u32[]{:S(2)}, u32[]{:S(2)}) collective-permute-start(f32[64,128]{1,0:T(8,128)S(1)} %get-tuple-element.262), channel_id=1, source_target_pairs={{0,16},{16,32},{32,48},{48,0},{1,17},{17,33},{33,49},{49,1},{2,18}... | collective-permute-start | bytes 98312 | tf_op jit(solution)/shard_map/ppermute | solution.py:19
  128.3 22.6 %collective-permute-start.19 = (f32[64,128]{1,0:T(8,128)S(1)}, f32[64,128]{1,0:T(8,128)S(1)}, u32[]{:S(2)}, u32[]{:S(2)}) collective-permute-start(f32[64,128]{1,0:T(8,128)S(1)} %get-tuple-element.262), channel_id=1, source_target_pairs={{0,32},{16,48},{32,0},{48,16},{1,33},{17,49},{33,1},{49,17},{2,34}... | collective-permute-start | bytes 98312 | tf_op jit(solution)/shard_map/ppermute | solution.py:19
  130.5 20.4 %collective-permute-start.20 = (f32[64,128]{1,0:T(8,128)S(1)}, f32[64,128]{1,0:T(8,128)S(1)}, u32[]{:S(2)}, u32[]{:S(2)}) collective-permute-start(f32[64,128]{1,0:T(8,128)S(1)} %get-tuple-element.262), channel_id=1, source_target_pairs={{0,48},{16,0},{32,16},{48,32},{1,49},{17,1},{33,17},{49,33},{2,50}... | collective-permute-start | bytes 98312 | tf_op jit(solution)/shard_map/ppermute | solution.py:19
  153.5 19.7 %collective-permute-start.21 = (f32[64,128]{1,0:T(8,128)S(1)}, f32[64,128]{1,0:T(8,128)S(1)}, u32[]{:S(2)}, u32[]{:S(2)}) collective-permute-start(f32[64,128]{1,0:T(8,128)S(1)} %get-tuple-element.264), channel_id=1, source_target_pairs={{0,16},{16,32},{32,48},{48,0},{1,17},{17,33},{33,49},{49,1},{2,18}... | collective-permute-start | bytes 98312 | tf_op jit(solution)/shard_map/ppermute | solution.py:19
  153.6 19.6 %collective-permute-start.22 = (f32[64,128]{1,0:T(8,128)S(1)}, f32[64,128]{1,0:T(8,128)S(1)}, u32[]{:S(2)}, u32[]{:S(2)}) collective-permute-start(f32[64,128]{1,0:T(8,128)S(1)} %get-tuple-element.264), channel_id=1, source_target_pairs={{0,32},{16,48},{32,0},{48,16},{1,33},{17,49},{33,1},{49,17},{2,34}... | collective-permute-start | bytes 98312 | tf_op jit(solution)/shard_map/ppermute | solution.py:19
  175.8 23.0 %collective-permute-start.24 = (f32[64,128]{1,0:T(8,128)S(1)}, f32[64,128]{1,0:T(8,128)S(1)}, u32[]{:S(2)}, u32[]{:S(2)}) collective-permute-start(f32[64,128]{1,0:T(8,128)S(1)} %get-tuple-element.266), channel_id=1, source_target_pairs={{0,16},{16,32},{32,48},{48,0},{1,17},{17,33},{33,49},{49,1},{2,18}... | collective-permute-start | bytes 98312 | tf_op jit(solution)/shard_map/ppermute | solution.py:19
  176.2 22.6 %collective-permute-start.25 = (f32[64,128]{1,0:T(8,128)S(1)}, f32[64,128]{1,0:T(8,128)S(1)}, u32[]{:S(2)}, u32[]{:S(2)}) collective-permute-start(f32[64,128]{1,0:T(8,128)S(1)} %get-tuple-element.266), channel_id=1, source_target_pairs={{0,32},{16,48},{32,0},{48,16},{1,33},{17,49},{33,1},{49,17},{2,34}... | collective-permute-start | bytes 98312 | tf_op jit(solution)/shard_map/ppermute | solution.py:19
  178.4 20.4 %collective-permute-start.26 = (f32[64,128]{1,0:T(8,128)S(1)}, f32[64,128]{1,0:T(8,128)S(1)}, u32[]{:S(2)}, u32[]{:S(2)}) collective-permute-start(f32[64,128]{1,0:T(8,128)S(1)} %get-tuple-element.266), channel_id=1, source_target_pairs={{0,48},{16,0},{32,16},{48,32},{1,49},{17,1},{33,17},{49,33},{2,50}... | collective-permute-start | bytes 98312 | tf_op jit(solution)/shard_map/ppermute | solution.py:19
  205.5 21.0 %all-to-all-start = ((f32[16,64,128]{2,1,0:T(8,128)}), f32[16,64,128]{2,1,0:T(8,128)S(1)}, u32[]{:S(2)}, u32[]{:S(2)}) async-start(f32[16,64,128]{2,1,0:T(8,128)} %select_reduce_fusion.20), calls=%async_computation | async-start | bytes 1048576 | tf_op jit(solution)/shard_map/while/body/eval_jaxpr/all_to_all | solution.py:41
  230.5 20.2 %all-to-all-start = ((f32[16,64,128]{2,1,0:T(8,128)}), f32[16,64,128]{2,1,0:T(8,128)S(1)}, u32[]{:S(2)}, u32[]{:S(2)}) async-start(f32[16,64,128]{2,1,0:T(8,128)} %select_reduce_fusion.20), calls=%async_computation | async-start | bytes 1048576 | tf_op jit(solution)/shard_map/while/body/eval_jaxpr/all_to_all | solution.py:41
  254.7 20.2 %all-to-all-start = ((f32[16,64,128]{2,1,0:T(8,128)}), f32[16,64,128]{2,1,0:T(8,128)S(1)}, u32[]{:S(2)}, u32[]{:S(2)}) async-start(f32[16,64,128]{2,1,0:T(8,128)} %select_reduce_fusion.20), calls=%async_computation | async-start | bytes 1048576 | tf_op jit(solution)/shard_map/while/body/eval_jaxpr/all_to_all | solution.py:41
  278.9 20.2 %all-to-all-start = ((f32[16,64,128]{2,1,0:T(8,128)}), f32[16,64,128]{2,1,0:T(8,128)S(1)}, u32[]{:S(2)}, u32[]{:S(2)}) async-start(f32[16,64,128]{2,1,0:T(8,128)} %select_reduce_fusion.20), calls=%async_computation | async-start | bytes 1048576 | tf_op jit(solution)/shard_map/while/body/eval_jaxpr/all_to_all | solution.py:41
  303.0 20.2 %all-to-all-start = ((f32[16,64,128]{2,1,0:T(8,128)}), f32[16,64,128]{2,1,0:T(8,128)S(1)}, u32[]{:S(2)}, u32[]{:S(2)}) async-start(f32[16,64,128]{2,1,0:T(8,128)} %select_reduce_fusion.20), calls=%async_computation | async-start | bytes 1048576 | tf_op jit(solution)/shard_map/while/body/eval_jaxpr/all_to_all | solution.py:41
  327.2 20.2 %all-to-all-start = ((f32[16,64,128]{2,1,0:T(8,128)}), f32[16,64,128]{2,1,0:T(8,128)S(1)}, u32[]{:S(2)}, u32[]{:S(2)}) async-start(f32[16,64,128]{2,1,0:T(8,128)} %select_reduce_fusion.20), calls=%async_computation | async-start | bytes 1048576 | tf_op jit(solution)/shard_map/while/body/eval_jaxpr/all_to_all | solution.py:41
  351.4 20.2 %all-to-all-start = ((f32[16,64,128]{2,1,0:T(8,128)}), f32[16,64,128]{2,1,0:T(8,128)S(1)}, u32[]{:S(2)}, u32[]{:S(2)}) async-start(f32[16,64,128]{2,1,0:T(8,128)} %select_reduce_fusion.20), calls=%async_computation | async-start | bytes 1048576 | tf_op jit(solution)/shard_map/while/body/eval_jaxpr/all_to_all | solution.py:41
  (34 other events, 498.5 us)
where the time goes:
time: 381 us; the launch traced here: 379 us
  blocking collectives  128 us (34%)
  waiting for transfers between devices  115 us (30%)
  starting transfers between devices  68.4 us (18%)
  matrix products  52.2 us (14%)
  other arithmetic  11.9 us (3%)
    all_gather x7, blocking collectives, gather_sources(): by_col = lax.all_gather(block[None], 'col', axis=0, tiled=True)  128 us
    all_to_all x7, waiting for transfers between devices, push_back(): incoming = lax.all_to_all(slots, 'col', 0, 0, tiled=True).sum(0)  106 us
    ppermute x45, starting transfers between devices, shifted(): return lax.ppermute(value, axis, [(i, (i + k) % n) for i in range(n)])  43.7 us
    all_to_all x7, starting transfers between devices, push_back(): incoming = lax.all_to_all(slots, 'col', 0, 0, tiled=True).sum(0)  24.6 us
    dot_general x8, matrix products, apply_transpose(): return jnp.einsum('rs,st->rt', block, inverse, precision=highest)  12.8 us
    ppermute x45, waiting for transfers between devices, shifted(): return lax.ppermute(value, axis, [(i, (i + k) % n) for i in range(n)])  9.6 us
    dot_general x7, matrix products, solve_top(): jnp.einsum('jrs,jts->rt', picked, top_blocks[height - 1], precision=highest)  9.58 us
    dot_general x8, matrix products, apply_inverse(): return jnp.einsum('rs,ts->rt', block, inverse, precision=highest)  8.76 us
  transfers between devices with their start and end apart: 52, of which 9 were waited for; matrix products, arithmetic and copies ran while one was open for 1% of the time, Pallas kernels for 0%

commit v1 on v0

--- a/solution.py
+++ b/solution.py
@@ -29,7 +29,9 @@
 
 
 def gather_sources(block, col_pick, row_pick):
-    by_col = lax.all_gather(block[None], "col", axis=0, tiled=True)
+    by_col = jnp.concatenate(
+        lax.all_to_all(jnp.stack([block[None]] * lax.axis_size("col")), "col", 0, 0), axis=0
+    )
     n_row = lax.axis_size("row")
     by_shift = jnp.stack([block] + [shifted(block, "row", k) for k in range(1, n_row)])
     return select_sum(col_pick, by_col) + select_sum(row_pick, by_shift)

time: 381 us -> 388 us (1.018)
  blocking collectives: 128 us -> 0 us
  waiting for transfers between devices: 115 us -> 175 us
  starting transfers between devices: 68.4 us -> 123 us
  other arithmetic: 11.9 us -> 19.8 us
  local copies, waits for them, and re-layouts: 1.48 us -> 8.58 us
  matrix products: 52.2 us -> 56.8 us
    all_gather x7 -> x0, blocking collectives: 128 us -> none  [gather_sources(): by_col = lax.all_gather(block[None], 'col', axis=0, tiled=True)]
    all_to_all x0 -> x7, waiting for transfers between devices: none -> 63 us  [gather_sources(): lax.all_to_all(jnp.stack([block[None]] * lax.axis_size('col')), 'col', 0, 0)]
    all_to_all x0 -> x7, starting transfers between devices: none -> 30.8 us  [gather_sources(): lax.all_to_all(jnp.stack([block[None]] * lax.axis_size('col')), 'col', 0, 0)]
    ppermute x45, starting transfers between devices: 43.7 us -> 68.1 us  [shifted(): return lax.ppermute(value, axis, [(i, (i + k) % n) for i in range(n)])]
    all_to_all x7, waiting for transfers between devices: 106 us -> 89 us  [push_back(): incoming = lax.all_to_all(slots, 'col', 0, 0, tiled=True).sum(0)]
    ppermute x45, waiting for transfers between devices: 9.6 us -> 23.2 us  [shifted(): return lax.ppermute(value, axis, [(i, (i + k) % n) for i in range(n)])]
    reduce_sum x15, other arithmetic: 2.55 us -> 10.4 us  [select_sum(): return jnp.sum(jnp.where(mask, stacked[None], 0.0), axis=1)]
    another operation x0 -> x7, local copies, waits for them, and re-layouts: none -> 5.91 us  [gather_sources(): jnp.stack([block[None]] * lax.axis_size('col'))]
  transfers between devices with their start and end apart: 52 -> 59, of which waited for: 9 -> 30; matrix products, arithmetic and copies ran while one was open for 1% -> 2% of each run, Pallas kernels for 0% -> 0%
where the time goes in v1:
time: 388 us; the launch traced here: 385 us
  waiting for transfers between devices  175 us (45%)
  starting transfers between devices  123 us (32%)
  matrix products  56.8 us (15%)
  other arithmetic  19.8 us (5%)
  local copies, waits for them, and re-layouts  8.58 us (2%)
    all_to_all x7, waiting for transfers between devices, push_back(): incoming = lax.all_to_all(slots, 'col', 0, 0, tiled=True).sum(0)  89 us
    ppermute x45, starting transfers between devices, shifted(): return lax.ppermute(value, axis, [(i, (i + k) % n) for i in range(n)])  68.1 us
    all_to_all x7, waiting for transfers between devices, gather_sources(): lax.all_to_all(jnp.stack([block[None]] * lax.axis_size('col')), 'col', 0, 0)  63 us
    all_to_all x7, starting transfers between devices, gather_sources(): lax.all_to_all(jnp.stack([block[None]] * lax.axis_size('col')), 'col', 0, 0)  30.8 us
    all_to_all x7, starting transfers between devices, push_back(): incoming = lax.all_to_all(slots, 'col', 0, 0, tiled=True).sum(0)  24.3 us
    ppermute x45, waiting for transfers between devices, shifted(): return lax.ppermute(value, axis, [(i, (i + k) % n) for i in range(n)])  23.2 us
    dot_general x8, matrix products, apply_inverse(): return jnp.einsum('rs,ts->rt', block, inverse, precision=highest)  13.6 us
    dot_general x8, matrix products, apply_transpose(): return jnp.einsum('rs,st->rt', block, inverse, precision=highest)  12.7 us
  transfers between devices with their start and end apart: 59, of which 30 were waited for; matrix products, arithmetic and copies ran while one was open for 2% of the time, Pallas kernels for 0%

profile of v1, /device:TPU:1, one launch (start us, length us, event | category | flops | bytes accessed | tf_op | source)
XLA Modules:
  0.0 385.1 jit_solution(2503083402978063796)
XLA Ops:
  0.6 3.7 fusion.37
  14.9 8.8 %collective-permute-done.4 = f32[8,64,128]{2,0,1:T(8,128)S(1)} collective-permute-done((f32[8,64,128]{2,0,1:T(8,128)S(1)}, f32[8,64,128]{2,0,1:T(8,128)S(1)}, u32[]{:S(2)}, u32[]{:S(2)}) %collective-permute-start.4) | collective-permute-done | bytes 262176 | tf_op jit(solution)/shard_map/ppermute | solution.py:19
  27.9 10.0 %all-to-all-start.1 = ((f32[16,1,64,128]{3,2,1,0:T(8,128)}), f32[16,1,64,128]{3,2,1,0:T(8,128)S(1)}, u32[]{:S(2)}, u32[]{:S(2)}) async-start(f32[16,1,64,128]{3,2,1,0:T(8,128)} %stack.159), calls=%async_computation.1 | async-start | bytes 1048576 | tf_op jit(solution)/shard_map/all_to_all | solution.py:33
  45.9 9.2 %all-to-all-done.1 = f32[16,1,64,128]{3,2,1,0:T(8,128)S(1)} async-done(((f32[16,1,64,128]{3,2,1,0:T(8,128)}), f32[16,1,64,128]{3,2,1,0:T(8,128)S(1)}, u32[]{:S(2)}, u32[]{:S(2)}) %all-to-all-start.1) | async-done | bytes 524320 | tf_op jit(solution)/shard_map/all_to_all | solution.py:33
  71.2 8.8 %all-to-all-done.2 = f32[16,1,64,128]{3,2,1,0:T(8,128)S(1)} async-done(((f32[16,1,64,128]{3,2,1,0:T(8,128)}), f32[16,1,64,128]{3,2,1,0:T(8,128)S(1)}, u32[]{:S(2)}, u32[]{:S(2)}) %all-to-all-start.2) | async-done | bytes 524320 | tf_op jit(solution)/shard_map/all_to_all | solution.py:33
  84.8 3.5 all-to-all-start.3
  96.1 8.9 %all-to-all-done.3 = f32[16,1,64,128]{3,2,1,0:T(8,128)S(1)} async-done(((f32[16,1,64,128]{3,2,1,0:T(8,128)}), f32[16,1,64,128]{3,2,1,0:T(8,128)S(1)}, u32[]{:S(2)}, u32[]{:S(2)}) %all-to-all-start.3) | async-done | bytes 524320 | tf_op jit(solution)/shard_map/all_to_all | solution.py:33
  109.7 3.5 all-to-all-start.4
  121.1 8.9 %all-to-all-done.4 = f32[16,1,64,128]{3,2,1,0:T(8,128)S(1)} async-done(((f32[16,1,64,128]{3,2,1,0:T(8,128)}), f32[16,1,64,128]{3,2,1,0:T(8,128)S(1)}, u32[]{:S(2)}, u32[]{:S(2)}) %all-to-all-start.4) | async-done | bytes 524320 | tf_op jit(solution)/shard_map/all_to_all | solution.py:33
  134.7 3.5 all-to-all-start.5
  146.0 8.8 %all-to-all-done.5 = f32[16,1,64,128]{3,2,1,0:T(8,128)S(1)} async-done(((f32[16,1,64,128]{3,2,1,0:T(8,128)}), f32[16,1,64,128]{3,2,1,0:T(8,128)S(1)}, u32[]{:S(2)}, u32[]{:S(2)}) %all-to-all-start.5) | async-done | bytes 524320 | tf_op jit(solution)/shard_map/all_to_all | solution.py:33
  159.7 3.5 all-to-all-start.6
  170.9 8.9 %all-to-all-done.6 = f32[16,1,64,128]{3,2,1,0:T(8,128)S(1)} async-done(((f32[16,1,64,128]{3,2,1,0:T(8,128)}), f32[16,1,64,128]{3,2,1,0:T(8,128)S(1)}, u32[]{:S(2)}, u32[]{:S(2)}) %all-to-all-start.6) | async-done | bytes 524320 | tf_op jit(solution)/shard_map/all_to_all | solution.py:33
  195.2 9.5 %all-to-all-done.7 = f32[16,1,64,128]{3,2,1,0:T(8,128)S(1)} async-done(((f32[16,1,64,128]{3,2,1,0:T(8,128)}), f32[16,1,64,128]{3,2,1,0:T(8,128)S(1)}, u32[]{:S(2)}, u32[]{:S(2)}) %all-to-all-start.7) | async-done | bytes 524320 | tf_op jit(solution)/shard_map/all_to_all | solution.py:33
  210.4 169.2 %while.18 = (s32[]{:T(128)}, f32[64,128]{1,0:T(8,128)S(1)}, f32[8,64,128]{2,1,0:T(8,128)}, f32[8,64,128]{2,1,0:T(8,128)}, pred[7,4,16]{2,1,0:T(4,128)(4,1)S(1)},...) while((s32[]{:T(128)}, f32[64,128]{1,0:T(8,128)S(1)}, ...), condition=%wide.region_19.20_spmd, body=%wide.region_15.19_spmd.sunk | while | flops 64225288 | bytes 4393060 | solution.py:85
  220.2 12.7 %all-to-all-done = f32[16,64,128]{2,1,0:T(8,128)S(1)} async-done(((f32[16,64,128]{2,1,0:T(8,128)}), f32[16,64,128]{2,1,0:T(8,128)S(1)}, u32[]{:S(2)}, u32[]{:S(2)}) %all-to-all-start) | async-done | bytes 524320 | tf_op jit(solution)/shard_map/while/body/eval_jaxpr/all_to_all | solution.py:43
  236.9 3.5 all-to-all-start
  244.3 12.7 %all-to-all-done = f32[16,64,128]{2,1,0:T(8,128)S(1)} async-done(((f32[16,64,128]{2,1,0:T(8,128)}), f32[16,64,128]{2,1,0:T(8,128)S(1)}, u32[]{:S(2)}, u32[]{:S(2)}) %all-to-all-start) | async-done | bytes 524320 | tf_op jit(solution)/shard_map/while/body/eval_jaxpr/all_to_all | solution.py:43
  261.0 3.5 all-to-all-start
  268.5 12.7 %all-to-all-done = f32[16,64,128]{2,1,0:T(8,128)S(1)} async-done(((f32[16,64,128]{2,1,0:T(8,128)}), f32[16,64,128]{2,1,0:T(8,128)S(1)}, u32[]{:S(2)}, u32[]{:S(2)}) %all-to-all-start) | async-done | bytes 524320 | tf_op jit(solution)/shard_map/while/body/eval_jaxpr/all_to_all | solution.py:43
  292.7 12.7 %all-to-all-done = f32[16,64,128]{2,1,0:T(8,128)S(1)} async-done(((f32[16,64,128]{2,1,0:T(8,128)}), f32[16,64,128]{2,1,0:T(8,128)S(1)}, u32[]{:S(2)}, u32[]{:S(2)}) %all-to-all-start) | async-done | bytes 524320 | tf_op jit(solution)/shard_map/while/body/eval_jaxpr/all_to_all | solution.py:43
  316.9 12.7 %all-to-all-done = f32[16,64,128]{2,1,0:T(8,128)S(1)} async-done(((f32[16,64,128]{2,1,0:T(8,128)}), f32[16,64,128]{2,1,0:T(8,128)S(1)}, u32[]{:S(2)}, u32[]{:S(2)}) %all-to-all-start) | async-done | bytes 524320 | tf_op jit(solution)/shard_map/while/body/eval_jaxpr/all_to_all | solution.py:43
  341.0 12.7 %all-to-all-done = f32[16,64,128]{2,1,0:T(8,128)S(1)} async-done(((f32[16,64,128]{2,1,0:T(8,128)}), f32[16,64,128]{2,1,0:T(8,128)S(1)}, u32[]{:S(2)}, u32[]{:S(2)}) %all-to-all-start) | async-done | bytes 524320 | tf_op jit(solution)/shard_map/while/body/eval_jaxpr/all_to_all | solution.py:43
  365.2 12.7 %all-to-all-done = f32[16,64,128]{2,1,0:T(8,128)S(1)} async-done(((f32[16,64,128]{2,1,0:T(8,128)}), f32[16,64,128]{2,1,0:T(8,128)S(1)}, u32[]{:S(2)}, u32[]{:S(2)}) %all-to-all-start) | async-done | bytes 524320 | tf_op jit(solution)/shard_map/while/body/eval_jaxpr/all_to_all | solution.py:43
  (226 shorter events, 188.3 us)
Async XLA Ops:
  27.9 27.2 %all-to-all-start.1 = ((f32[16,1,64,128]{3,2,1,0:T(8,128)}), f32[16,1,64,128]{3,2,1,0:T(8,128)S(1)}, u32[]{:S(2)}, u32[]{:S(2)}) async-start(f32[16,1,64,128]{3,2,1,0:T(8,128)} %stack.159), calls=%async_computation.1 | async-start | bytes 1048576 | tf_op jit(solution)/shard_map/all_to_all | solution.py:33
  59.9 20.2 %all-to-all-start.2 = ((f32[16,1,64,128]{3,2,1,0:T(8,128)}), f32[16,1,64,128]{3,2,1,0:T(8,128)S(1)}, u32[]{:S(2)}, u32[]{:S(2)}) async-start(f32[16,1,64,128]{3,2,1,0:T(8,128)} %stack.165), calls=%async_computation.2 | async-start | bytes 1048576 | tf_op jit(solution)/shard_map/all_to_all | solution.py:33
  84.8 20.2 %all-to-all-start.3 = ((f32[16,1,64,128]{3,2,1,0:T(8,128)}), f32[16,1,64,128]{3,2,1,0:T(8,128)S(1)}, u32[]{:S(2)}, u32[]{:S(2)}) async-start(f32[16,1,64,128]{3,2,1,0:T(8,128)} %stack.171), calls=%async_computation.3 | async-start | bytes 1048576 | tf_op jit(solution)/shard_map/all_to_all | solution.py:33
  109.7 20.2 %all-to-all-start.4 = ((f32[16,1,64,128]{3,2,1,0:T(8,128)}), f32[16,1,64,128]{3,2,1,0:T(8,128)S(1)}, u32[]{:S(2)}, u32[]{:S(2)}) async-start(f32[16,1,64,128]{3,2,1,0:T(8,128)} %stack.177), calls=%async_computation.4 | async-start | bytes 1048576 | tf_op jit(solution)/shard_map/all_to_all | solution.py:33
  134.7 20.2 %all-to-all-start.5 = ((f32[16,1,64,128]{3,2,1,0:T(8,128)}), f32[16,1,64,128]{3,2,1,0:T(8,128)S(1)}, u32[]{:S(2)}, u32[]{:S(2)}) async-start(f32[16,1,64,128]{3,2,1,0:T(8,128)} %stack.183), calls=%async_computation.5 | async-start | bytes 1048576 | tf_op jit(solution)/shard_map/all_to_all | solution.py:33
  159.7 20.2 %all-to-all-start.6 = ((f32[16,1,64,128]{3,2,1,0:T(8,128)}), f32[16,1,64,128]{3,2,1,0:T(8,128)S(1)}, u32[]{:S(2)}, u32[]{:S(2)}) async-start(f32[16,1,64,128]{3,2,1,0:T(8,128)} %stack.189), calls=%async_computation.6 | async-start | bytes 1048576 | tf_op jit(solution)/shard_map/all_to_all | solution.py:33
  184.6 20.2 %all-to-all-start.7 = ((f32[16,1,64,128]{3,2,1,0:T(8,128)}), f32[16,1,64,128]{3,2,1,0:T(8,128)S(1)}, u32[]{:S(2)}, u32[]{:S(2)}) async-start(f32[16,1,64,128]{3,2,1,0:T(8,128)} %stack.195), calls=%async_computation.7 | async-start | bytes 1048576 | tf_op jit(solution)/shard_map/all_to_all | solution.py:33
  212.7 20.2 %all-to-all-start = ((f32[16,64,128]{2,1,0:T(8,128)}), f32[16,64,128]{2,1,0:T(8,128)S(1)}, u32[]{:S(2)}, u32[]{:S(2)}) async-start(f32[16,64,128]{2,1,0:T(8,128)} %select_reduce_fusion.20), calls=%async_computation | async-start | bytes 1048576 | tf_op jit(solution)/shard_map/while/body/eval_jaxpr/all_to_all | solution.py:43
  216.3 16.6 %collective-permute-start = (f32[64,128]{1,0:T(8,128)S(1)}, f32[64,128]{1,0:T(8,128)S(1)}, u32[]{:S(2)}, u32[]{:S(2)}) collective-permute-start(f32[64,128]{1,0:T(8,128)S(1)} %get-tuple-element.323), channel_id=1, source_target_pairs={{0,48},{16,0},{32,16},{48,32},{1,49},{17,1},{33,17},{49,33},{2,50}... | collective-permute-start | bytes 98312 | tf_op jit(solution)/shard_map/while/body/eval_jaxpr/ppermute | solution.py:19
  219.1 13.8 %collective-permute-start.1 = (f32[64,128]{1,0:T(8,128)S(1)}, f32[64,128]{1,0:T(8,128)S(1)}, u32[]{:S(2)}, u32[]{:S(2)}) collective-permute-start(f32[64,128]{1,0:T(8,128)S(1)} %get-tuple-element.324), channel_id=1, source_target_pairs={{0,32},{16,48},{32,0},{48,16},{1,33},{17,49},{33,1},{49,17},{2,34}... | collective-permute-start | bytes 98312 | tf_op jit(solution)/shard_map/while/body/eval_jaxpr/ppermute | solution.py:19
  236.9 20.2 %all-to-all-start = ((f32[16,64,128]{2,1,0:T(8,128)}), f32[16,64,128]{2,1,0:T(8,128)S(1)}, u32[]{:S(2)}, u32[]{:S(2)}) async-start(f32[16,64,128]{2,1,0:T(8,128)} %select_reduce_fusion.20), calls=%async_computation | async-start | bytes 1048576 | tf_op jit(solution)/shard_map/while/body/eval_jaxpr/all_to_all | solution.py:43
  240.5 16.6 %collective-permute-start = (f32[64,128]{1,0:T(8,128)S(1)}, f32[64,128]{1,0:T(8,128)S(1)}, u32[]{:S(2)}, u32[]{:S(2)}) collective-permute-start(f32[64,128]{1,0:T(8,128)S(1)} %get-tuple-element.323), channel_id=1, source_target_pairs={{0,48},{16,0},{32,16},{48,32},{1,49},{17,1},{33,17},{49,33},{2,50}... | collective-permute-start | bytes 98312 | tf_op jit(solution)/shard_map/while/body/eval_jaxpr/ppermute | solution.py:19
  261.0 20.2 %all-to-all-start = ((f32[16,64,128]{2,1,0:T(8,128)}), f32[16,64,128]{2,1,0:T(8,128)S(1)}, u32[]{:S(2)}, u32[]{:S(2)}) async-start(f32[16,64,128]{2,1,0:T(8,128)} %select_reduce_fusion.20), calls=%async_computation | async-start | bytes 1048576 | tf_op jit(solution)/shard_map/while/body/eval_jaxpr/all_to_all | solution.py:43
  264.7 16.6 %collective-permute-start = (f32[64,128]{1,0:T(8,128)S(1)}, f32[64,128]{1,0:T(8,128)S(1)}, u32[]{:S(2)}, u32[]{:S(2)}) collective-permute-start(f32[64,128]{1,0:T(8,128)S(1)} %get-tuple-element.323), channel_id=1, source_target_pairs={{0,48},{16,0},{32,16},{48,32},{1,49},{17,1},{33,17},{49,33},{2,50}... | collective-permute-start | bytes 98312 | tf_op jit(solution)/shard_map/while/body/eval_jaxpr/ppermute | solution.py:19
  285.2 20.2 %all-to-all-start = ((f32[16,64,128]{2,1,0:T(8,128)}), f32[16,64,128]{2,1,0:T(8,128)S(1)}, u32[]{:S(2)}, u32[]{:S(2)}) async-start(f32[16,64,128]{2,1,0:T(8,128)} %select_reduce_fusion.20), calls=%async_computation | async-start | bytes 1048576 | tf_op jit(solution)/shard_map/while/body/eval_jaxpr/all_to_all | solution.py:43
  288.8 16.6 %collective-permute-start = (f32[64,128]{1,0:T(8,128)S(1)}, f32[64,128]{1,0:T(8,128)S(1)}, u32[]{:S(2)}, u32[]{:S(2)}) collective-permute-start(f32[64,128]{1,0:T(8,128)S(1)} %get-tuple-element.323), channel_id=1, source_target_pairs={{0,48},{16,0},{32,16},{48,32},{1,49},{17,1},{33,17},{49,33},{2,50}... | collective-permute-start | bytes 98312 | tf_op jit(solution)/shard_map/while/body/eval_jaxpr/ppermute | solution.py:19
  309.4 20.2 %all-to-all-start = ((f32[16,64,128]{2,1,0:T(8,128)}), f32[16,64,128]{2,1,0:T(8,128)S(1)}, u32[]{:S(2)}, u32[]{:S(2)}) async-start(f32[16,64,128]{2,1,0:T(8,128)} %select_reduce_fusion.20), calls=%async_computation | async-start | bytes 1048576 | tf_op jit(solution)/shard_map/while/body/eval_jaxpr/all_to_all | solution.py:43
  313.0 16.6 %collective-permute-start = (f32[64,128]{1,0:T(8,128)S(1)}, f32[64,128]{1,0:T(8,128)S(1)}, u32[]{:S(2)}, u32[]{:S(2)}) collective-permute-start(f32[64,128]{1,0:T(8,128)S(1)} %get-tuple-element.323), channel_id=1, source_target_pairs={{0,48},{16,0},{32,16},{48,32},{1,49},{17,1},{33,17},{49,33},{2,50}... | collective-permute-start | bytes 98312 | tf_op jit(solution)/shard_map/while/body/eval_jaxpr/ppermute | solution.py:19
  315.8 13.8 %collective-permute-start.1 = (f32[64,128]{1,0:T(8,128)S(1)}, f32[64,128]{1,0:T(8,128)S(1)}, u32[]{:S(2)}, u32[]{:S(2)}) collective-permute-start(f32[64,128]{1,0:T(8,128)S(1)} %get-tuple-element.324), channel_id=1, source_target_pairs={{0,32},{16,48},{32,0},{48,16},{1,33},{17,49},{33,1},{49,17},{2,34}... | collective-permute-start | bytes 98312 | tf_op jit(solution)/shard_map/while/body/eval_jaxpr/ppermute | solution.py:19
  333.6 20.2 %all-to-all-start = ((f32[16,64,128]{2,1,0:T(8,128)}), f32[16,64,128]{2,1,0:T(8,128)S(1)}, u32[]{:S(2)}, u32[]{:S(2)}) async-start(f32[16,64,128]{2,1,0:T(8,128)} %select_reduce_fusion.20), calls=%async_computation | async-start | bytes 1048576 | tf_op jit(solution)/shard_map/while/body/eval_jaxpr/all_to_all | solution.py:43
  337.2 16.6 %collective-permute-start = (f32[64,128]{1,0:T(8,128)S(1)}, f32[64,128]{1,0:T(8,128)S(1)}, u32[]{:S(2)}, u32[]{:S(2)}) collective-permute-start(f32[64,128]{1,0:T(8,128)S(1)} %get-tuple-element.323), channel_id=1, source_target_pairs={{0,48},{16,0},{32,16},{48,32},{1,49},{17,1},{33,17},{49,33},{2,50}... | collective-permute-start | bytes 98312 | tf_op jit(solution)/shard_map/while/body/eval_jaxpr/ppermute | solution.py:19
  357.7 20.2 %all-to-all-start = ((f32[16,64,128]{2,1,0:T(8,128)}), f32[16,64,128]{2,1,0:T(8,128)S(1)}, u32[]{:S(2)}, u32[]{:S(2)}) async-start(f32[16,64,128]{2,1,0:T(8,128)} %select_reduce_fusion.20), calls=%async_computation | async-start | bytes 1048576 | tf_op jit(solution)/shard_map/while/body/eval_jaxpr/all_to_all | solution.py:43
  361.4 16.6 %collective-permute-start = (f32[64,128]{1,0:T(8,128)S(1)}, f32[64,128]{1,0:T(8,128)S(1)}, u32[]{:S(2)}, u32[]{:S(2)}) collective-permute-start(f32[64,128]{1,0:T(8,128)S(1)} %get-tuple-element.323), channel_id=1, source_target_pairs={{0,48},{16,0},{32,16},{48,32},{1,49},{17,1},{33,17},{49,33},{2,50}... | collective-permute-start | bytes 98312 | tf_op jit(solution)/shard_map/while/body/eval_jaxpr/ppermute | solution.py:19
  364.2 13.8 %collective-permute-start.1 = (f32[64,128]{1,0:T(8,128)S(1)}, f32[64,128]{1,0:T(8,128)S(1)}, u32[]{:S(2)}, u32[]{:S(2)}) collective-permute-start(f32[64,128]{1,0:T(8,128)S(1)} %get-tuple-element.324), channel_id=1, source_target_pairs={{0,32},{16,48},{32,0},{48,16},{1,33},{17,49},{33,1},{49,17},{2,34}... | collective-permute-start | bytes 98312 | tf_op jit(solution)/shard_map/while/body/eval_jaxpr/ppermute | solution.py:19
  (39 other events, 292.1 us)
